TPU v7x, 512 devices: a whole 4x4x16 slice. The times are simulated.
512 devices in a mesh: tile: 64 (over z, x_hi, core), chan: 8 (over x_lo, y).
Axes of the slice: x: 4 (x_hi: 2, x_lo: 2; x = x_hi * 2 + x_lo), y: 4, z: 16, core: 2. Of those that a mesh axis runs over, the one named last changes fastest.
Arguments:
- analysis: bfloat16 [64, 524288], P('chan', 'tile'), may hold values from -6 to 6
- send_rows: int32 [64, 5, 128], P('tile'), may hold values from 0 to 8191
- send_count: int32 [64, 5], P('tile'), may hold values from 64 to 128, as said below
- corner_slot: int32 [4, 2048, 256], P(None, 'tile'), may hold values from 0 to 639, as said below
- corner_weight: float32 [4, 2048, 256], P(None, 'tile'), may hold values from 0.1 to 0.6
- beside: int32 [2048, 8], P('tile'), may hold values from 0 to 2047, as said below
- quarter_turns: int32 [2048, 8], P('tile'), may hold values from 0 to 3
- kernel_one: bfloat16 [9, 128, 64], P(None, 'chan'), may hold values from -0.375 to 0.375
- kernel_two: bfloat16 [9, 128, 128], P(None, 'chan'), may hold values from -0.25 to 0.25
- kernel_three: bfloat16 [9, 128, 128], P(None, 'chan'), may hold values from -0.25 to 0.25
Outputs:
- forecast: bfloat16 [128, 2048, 256], P('chan', 'tile')
Inputs may be any that keep to these rules, and one draw needn't show every extreme that they name: send_count[s, d] is at least 64; every shard sends 128 to itself (d = 2), and some receiver gets 128 from each of its 5 senders. corner_slot[j, t, i] = d * 128 + k names a live slot, k < send_count[s, d], of the block that shard s = (e - d + 2) mod the shard count sends to the shard e holding tile t; the four corners of a pixel are slots k, k + 1, k + 2, k + 3 of one block. beside[t, k] = (t + d) mod 2048 with 1 <= |d| <= 2.
All inputs are finite; a program needn't handle non-finite values.
Results may differ from a plain program's by a relative error of at most 0.007.
Values may be sent and summed in bfloat16 or wider, within the bound.
No kernel may reach another device: no remote copies, remote signals or barrier semaphores. Data moves between devices by JAX's collectives and lax.ppermute only.
A program may use at most 64 MiB of HBM per device.

v0:
```python
import jax
import jax.numpy as jnp
import numpy as np
from jax import lax
from jax.sharding import PartitionSpec as P

P_SIZE = 16
REACH = 2


def from_behind(value, axis, steps):
    count = lax.axis_size(axis)
    pairs = [(source, (source + steps) % count) for source in range(count)]
    return lax.ppermute(value, axis, pairs)


def extended_2(x, sides, width):
    for axis, dim in sides:
        size, length = (lax.axis_size(axis), x.shape[dim])
        up = [(i, (i + 1) % size) for i in range(size)]
        down = [(j, i) for i, j in up]
        last = lax.slice_in_dim(x, length - width, length, axis=dim)
        initial = lax.slice_in_dim(x, 0, width, axis=dim)
        before = lax.ppermute(last, axis, up)
        after = lax.ppermute(initial, axis, down)
        x = jnp.concatenate([before, x, after], axis=dim)
    return x


def cycle_table(extent):
    length = 4 * extent - 4
    entries = []
    for cycle_pos in range(length):
        if cycle_pos < extent:
            row_at, col_at = (cycle_pos, 0)
        elif cycle_pos < 2 * extent - 1:
            row_at, col_at = (extent - 1, cycle_pos - extent + 1)
        elif cycle_pos < 3 * extent - 2:
            row_at, col_at = (3 * extent - 3 - cycle_pos, extent - 1)
        else:
            row_at, col_at = (0, 4 * extent - 4 - cycle_pos)
        entries.append(row_at * extent + col_at)
    return np.array(entries, np.int32)


def border_tables(extent):
    length = 4 * extent - 4
    heading = []
    anchor = []
    for col_at in range(extent):
        heading.append(0)
        anchor.append(extent - 1 + col_at)
    for col_at in range(extent):
        heading.append(1)
        anchor.append((length - col_at) % length)
    for row_at in range(extent):
        heading.append(2)
        anchor.append(3 * extent - 3 - row_at)
    for row_at in range(extent):
        heading.append(3)
        anchor.append(row_at)
    heading += [4, 5, 6, 7]
    anchor += [2 * extent - 2, extent - 1, 3 * extent - 3, 0]
    return (np.array(heading, np.int32), np.array(anchor, np.int32))


def layout_table(extent):
    padded_side = extent + 2
    interior = extent * extent
    entries = []
    for row_at in range(padded_side):
        for col_at in range(padded_side):
            if 1 <= row_at <= extent and 1 <= col_at <= extent:
                entries.append((row_at - 1) * extent + col_at - 1)
            elif row_at == 0 and 1 <= col_at <= extent:
                entries.append(interior + col_at - 1)
            elif row_at == padded_side - 1 and 1 <= col_at <= extent:
                entries.append(interior + extent + col_at - 1)
            elif col_at == 0 and 1 <= row_at <= extent:
                entries.append(interior + 2 * extent + row_at - 1)
            elif col_at == padded_side - 1 and 1 <= row_at <= extent:
                entries.append(interior + 3 * extent + row_at - 1)
            else:
                corner = (0 if row_at == 0 else 2) + (0 if col_at == 0 else 1)
                entries.append(interior + 4 * extent + corner)
    return np.array(entries, np.int32)


def conv_layer(activity, kernel, local_beside, local_turns, gather_rims):
    length = 4 * P_SIZE - 4
    cycle_vals = jnp.take(activity, cycle_table(P_SIZE), axis=2)
    extended = gather_rims(cycle_vals)
    heading, anchor = border_tables(P_SIZE)
    near_tile = jnp.take(local_beside, heading, axis=1)
    near_turn = jnp.take(local_turns, heading, axis=1)
    source = near_tile * length + jnp.remainder(anchor[None, :] - near_turn * (P_SIZE - 1), length)
    flat_cycles = extended.reshape(extended.shape[0], -1)
    border = jnp.take(flat_cycles, source.reshape(-1), axis=1)
    border = border.reshape(activity.shape[0], activity.shape[1], 4 * P_SIZE + 4)
    joined = jnp.concatenate([activity, border], axis=2)
    padded = jnp.take(joined, layout_table(P_SIZE), axis=2)
    padded_side = P_SIZE + 2
    stretch = P_SIZE * padded_side - 2
    summed = None
    for tap_index in range(9):
        offset = padded_side + 1 + (tap_index // 3 - 1) * padded_side + (tap_index % 3 - 1)
        window = padded[:, :, offset : offset + stretch]
        partial_sum = jnp.einsum(
            "oc,ctq->otq", kernel[tap_index], window, preferred_element_type=jnp.float32
        )
        summed = partial_sum if summed is None else summed + partial_sum
    summed = jnp.pad(summed, ((0, 0), (0, 0), (0, 2)))
    summed = summed.reshape(summed.shape[0], summed.shape[1], P_SIZE, padded_side)[:, :, :, :P_SIZE]
    summed = summed.reshape(summed.shape[0], summed.shape[1], P_SIZE * P_SIZE)
    return jax.nn.gelu(summed, approximate=False).astype(jnp.bfloat16)


def on_device(
    analysis,
    send_rows,
    send_count,
    corner_slot,
    corner_weight,
    beside,
    quarter_turns,
    kernel_one,
    kernel_two,
    kernel_three,
):
    shards = lax.axis_size("tile")
    groups = lax.axis_size("chan")
    tiles_here = corner_slot.shape[1]
    near_count = send_rows.shape[1]
    capacity = send_rows.shape[2]
    channels_here = analysis.shape[0]
    total_tiles = tiles_here * shards
    slot_order = jnp.arange(capacity)
    blocks = []
    for offset_index in range(near_count):
        rows_list = send_rows[0, offset_index]
        count_here = send_count[0, offset_index]
        source_block = analysis
        if offset_index != REACH:
            packed = jnp.concatenate([rows_list, count_here[None]])
            packed = from_behind(packed, "tile", offset_index - REACH)
            rows_list = packed[:capacity]
            count_here = packed[capacity]
            source_block = from_behind(analysis, "tile", offset_index - REACH)
        piece = jnp.take(source_block, rows_list, axis=1)
        piece = jnp.where(slot_order[None, :] < count_here, piece, jnp.zeros((), piece.dtype))
        blocks.append(piece)
    arrived = jnp.concatenate(blocks, axis=1)
    values = jnp.take(arrived, corner_slot.reshape(-1), axis=1)
    values = values.reshape(channels_here, 4, tiles_here, corner_slot.shape[2]).astype(jnp.float32)
    regridded = jnp.sum(values * corner_weight[None], axis=1).astype(jnp.bfloat16)
    per_group = tiles_here // groups
    activity = lax.all_to_all(regridded, "chan", split_axis=1, concat_axis=0, tiled=True)
    kernels = (
        lax.all_gather(kernel_one, "chan", axis=1, tiled=True),
        lax.all_gather(kernel_two, "chan", axis=1, tiled=True),
        lax.all_gather(kernel_three, "chan", axis=1, tiled=True),
    )
    first_tile = lax.axis_index(("tile", "chan")) * per_group
    near_beside = lax.dynamic_slice_in_dim(beside, lax.axis_index("chan") * per_group, per_group, 0)
    near_turns = lax.dynamic_slice_in_dim(
        quarter_turns, lax.axis_index("chan") * per_group, per_group, 0
    )
    local_beside = jnp.remainder(near_beside - first_tile + REACH, total_tiles)

    def joined_rims(cycle_vals):
        return extended_2(cycle_vals, ((("tile", "chan"), 1),), REACH)

    for kernel in kernels:
        activity = conv_layer(activity, kernel, local_beside, near_turns, joined_rims)
    result = lax.all_to_all(activity, "chan", split_axis=0, concat_axis=1, tiled=True)
    return result


def solution(mesh):
    return jax.shard_map(
        on_device,
        mesh=mesh,
        in_specs=(
            P("chan", "tile"),
            P("tile", None, None),
            P("tile", None),
            P(None, "tile", None),
            P(None, "tile", None),
            P("tile", None),
            P("tile", None),
            P(None, "chan", None),
            P(None, "chan", None),
            P(None, "chan", None),
        ),
        out_specs=P("chan", "tile", None),
        check_vma=False,
    )
```

profile of v0, /device:TPU:2, one launch (start us, length us, event | category | flops | bytes accessed | tf_op | source)
XLA Modules:
  0.0 374.5 jit_solution(5830040270725615998)
XLA Ops:
  0.0 13.1 %collective-permute-start.1 = (bf16[8,8192]{1,0:T(8,128)(2,1)}, bf16[8,8192]{1,0:T(8,128)(2,1)S(1)}, u32[]{:S(2)}, u32[]{:S(2)}) collective-permute-start(bf16[8,8192]{1,0:T(8,128)(2,1)} %param.32), channel_id=1, source_target_pairs={{0,496},{8,504},{16,0},{24,8},{32,16},{40,24},{48,32},{56,40},{64,... | collective-permute-start | bytes 393224 | tf_op jit(solution)/shard_map/ppermute | solution.py:14
  13.1 2.5 collective-permute-start.3
  15.6 1.9 collective-permute-start.5
  17.5 4.0 %collective-permute-start.7 = (bf16[8,8192]{1,0:T(8,128)(2,1)}, bf16[8,8192]{1,0:T(8,128)(2,1)S(1)}, u32[]{:S(2)}, u32[]{:S(2)}) collective-permute-start(bf16[8,8192]{1,0:T(8,128)(2,1)} %param.32), channel_id=1, source_target_pairs={{0,16},{8,24},{16,32},{24,40},{32,48},{40,56},{48,64},{56,72},{64,... | collective-permute-start | bytes 393224 | tf_op jit(solution)/shard_map/ppermute | solution.py:14
  21.6 1.5 fusion.74
  24.3 5.4 %collective-permute-start = (s32[129]{0:T(256)S(1)}, s32[129]{0:T(256)S(1)}, u32[]{:S(2)}, u32[]{:S(2)}) collective-permute-start(s32[129]{0:T(256)S(1)} %pad_add_fusion), channel_id=1, source_target_pairs={{0,496},{8,504},{16,0},{24,8},{32,16},{40,24},{48,32},{56,40},{64,... | collective-permute-start | bytes 1556 | tf_op jit(solution)/shard_map/ppermute | solution.py:14
  39.0 1.8 copy.262
  41.5 4.6 %collective-permute-start.2 = (s32[129]{0:T(256)S(1)}, s32[129]{0:T(256)S(1)}, u32[]{:S(2)}, u32[]{:S(2)}) collective-permute-start(s32[129]{0:T(256)S(1)} %pad_add_fusion.1), channel_id=1, source_target_pairs={{0,504},{8,0},{16,8},{24,16},{32,24},{40,32},{48,40},{56,48},{64,5... | collective-permute-start | bytes 1556 | tf_op jit(solution)/shard_map/ppermute | solution.py:14
  47.4 4.1 %collective-permute-start.4 = (s32[129]{0:T(256)S(1)}, s32[129]{0:T(256)S(1)}, u32[]{:S(2)}, u32[]{:S(2)}) collective-permute-start(s32[129]{0:T(256)S(1)} %pad_add_fusion.2), channel_id=1, source_target_pairs={{0,8},{8,16},{16,24},{24,32},{32,40},{40,48},{48,56},{56,64},{64,7... | collective-permute-start | bytes 1556 | tf_op jit(solution)/shard_map/ppermute | solution.py:14
  52.7 3.2 collective-permute-done.4
  55.9 1.9 collective-permute-start.6
  59.0 6.0 %collective-permute-done.6 = s32[129]{0:T(256)S(1)} collective-permute-done((s32[129]{0:T(256)S(1)}, s32[129]{0:T(256)S(1)}, u32[]{:S(2)}, u32[]{:S(2)}) %collective-permute-start.6) | collective-permute-done | bytes 548 | tf_op jit(solution)/shard_map/ppermute | solution.py:14
  73.7 114.2 %gather_fusion = bf16[32768,8]{1,0:T(8,128)(2,1)} fusion(bf16[8,640]{0,1:T(8,128)(2,1)S(1)} %fusion.60, s32[32768]{0:T(1024)S(1)} %broadcast_clamp_fusion), kind=kCustom, calls=%fused_computation.13 | custom fusion | bytes 1179648 | tf_op jit(solution)/shard_map/jit(_take)/gather | solution.py:153
  187.9 13.0 %multiply_reduce_fusion = bf16[8,32,256]{0,2,1:T(8,128)(2,1)S(1)} fusion(f32[4,32,256]{2,1,0:T(8,128)S(1)} %copy-done.1, bf16[8,4,32,256]{0,3,2,1:T(8,128)(2,1)} %bitcast.254, pred[4,32,256]{2,1,0:T(8,128)(4,1)S(1)} %compare_and_fusion), kind=kLoop, calls=%fused_computation.17 | loop fusion | flops 983040 | bytes 819200 | tf_op jit(solution)/shard_map/reduce_sum | solution.py:155
  202.5 5.9 %all-to-all-start = ((bf16[8,32,256]{2,0,1:T(8,128)(2,1)}), bf16[8,32,256]{2,0,1:T(8,128)(2,1)S(1)}, u32[]{:S(2)}, u32[]{:S(2)}) async-start(bf16[8,32,256]{2,0,1:T(8,128)(2,1)} %copy.266), calls=%async_computation | async-start | bytes 262144 | tf_op jit(solution)/shard_map/all_to_all | solution.py:157
  208.5 5.2 %all-to-all-done = bf16[8,32,256]{2,0,1:T(8,128)(2,1)S(1)} async-done(((bf16[8,32,256]{2,0,1:T(8,128)(2,1)}), bf16[8,32,256]{2,0,1:T(8,128)(2,1)S(1)}, u32[]{:S(2)}, u32[]{:S(2)}) %all-to-all-start) | async-done | bytes 131104 | tf_op jit(solution)/shard_map/all_to_all | solution.py:157
  214.6 2.6 collective-permute-start.8
  217.3 5.3 %collective-permute-start.9 = (bf16[64,2,60]{0,1,2:T(2,128)(2,1)S(1)}, bf16[64,2,60]{0,1,2:T(2,128)(2,1)S(1)}, u32[]{:S(2)}, u32[]{:S(2)}) collective-permute-start(bf16[64,2,60]{0,1,2:T(2,128)(2,1)S(1)} %get-tuple-element.33), channel_id=1, source_target_pairs={{1,0},{2,1},{3,2},{4,3},{5,4},{6,5},{7,6},{8,7},{9,8},{10,9},{11,1... | collective-permute-start | bytes 46088 | tf_op jit(solution)/shard_map/ppermute | solution.py:25
  222.6 29.0 %all_gather.9 = bf16[9,128,64]{2,1,0:T(8,128)(2,1)S(1)} all-gather(bf16[9,16,64]{2,1,0:T(8,128)(2,1)S(1)} %copy-done.2), channel_id=1, replica_groups=mesh['tile'=64,'chan'=8] {'chan'}, dimensions={1}, use_global_device_ids=true | all-gather | bytes 165888 | tf_op jit(solution)/shard_map/all_gather | solution.py:159
  251.9 1.4 gather_fusion.2
  253.8 2.0 gather_fusion.3
  263.0 1.9 collective-permute-start.10
  264.9 6.0 %collective-permute-start.11 = (bf16[128,2,60]{0,1,2:T(2,128)(2,1)S(1)}, bf16[128,2,60]{0,1,2:T(2,128)(2,1)S(1)}, u32[]{:S(2)}, u32[]{:S(2)}) collective-permute-start(bf16[128,2,60]{0,1,2:T(2,128)(2,1)S(1)} %get-tuple-element.31), channel_id=1, source_target_pairs={{1,0},{2,1},{3,2},{4,3},{5,4},{6,5},{7,6},{8,7},{9,8},{10,9},{11,1... | collective-permute-start | bytes 92168 | tf_op jit(solution)/shard_map/ppermute | solution.py:25
  270.9 31.7 %all_gather.10 = bf16[9,128,128]{2,1,0:T(8,128)(2,1)S(1)} all-gather(bf16[9,16,128]{2,1,0:T(8,128)(2,1)S(1)} %copy-done.3), channel_id=1, replica_groups=mesh['tile'=64,'chan'=8] {'chan'}, dimensions={1}, use_global_device_ids=true | all-gather | bytes 331776 | tf_op jit(solution)/shard_map/all_gather | solution.py:160
  302.8 1.4 gather_fusion.12
  304.8 2.0 gather_fusion.13
  312.4 2.0 collective-permute-start.12
  314.4 5.9 %collective-permute-start.13 = (bf16[128,2,60]{0,1,2:T(2,128)(2,1)S(1)}, bf16[128,2,60]{0,1,2:T(2,128)(2,1)S(1)}, u32[]{:S(2)}, u32[]{:S(2)}) collective-permute-start(bf16[128,2,60]{0,1,2:T(2,128)(2,1)S(1)} %get-tuple-element.29), channel_id=1, source_target_pairs={{1,0},{2,1},{3,2},{4,3},{5,4},{6,5},{7,6},{8,7},{9,8},{10,9},{11,1... | collective-permute-start | bytes 92168 | tf_op jit(solution)/shard_map/ppermute | solution.py:25
  320.3 31.7 %all_gather.11 = bf16[9,128,128]{2,1,0:T(8,128)(2,1)S(1)} all-gather(bf16[9,16,128]{2,1,0:T(8,128)(2,1)S(1)} %copy-done.4), channel_id=1, replica_groups=mesh['tile'=64,'chan'=8] {'chan'}, dimensions={1}, use_global_device_ids=true | all-gather | bytes 331776 | tf_op jit(solution)/shard_map/all_gather | solution.py:161
  352.3 1.4 gather_fusion.15
  354.2 2.0 gather_fusion.16
  361.1 12.5 %all_to_all.36 = bf16[128,4,256]{2,1,0:T(4,128)(2,1)S(1)} all-to-all(bf16[128,4,256]{2,1,0:T(4,128)(2,1)S(1)} %copy.324), channel_id=1, replica_groups=mesh['tile'=64,'chan'=8] {'chan'}, dimensions={0} | all-to-all | bytes 524288 | tf_op jit(solution)/shard_map/all_to_all | solution.py:175
  (173 shorter events, 46.0 us)
Async XLA Ops:
  0.0 34.5 %copy-start = (s32[32,8]{0,1:T(8,128)S(1)}, s32[32,8]{0,1:T(8,128)}, u32[]{:S(2)}) copy-start(s32[32,8]{0,1:T(8,128)} %param.38) | copy-start | bytes 3076
  0.0 66.1 %collective-permute-start.1 = (bf16[8,8192]{1,0:T(8,128)(2,1)}, bf16[8,8192]{1,0:T(8,128)(2,1)S(1)}, u32[]{:S(2)}, u32[]{:S(2)}) collective-permute-start(bf16[8,8192]{1,0:T(8,128)(2,1)} %param.32), channel_id=1, source_target_pairs={{0,496},{8,504},{16,0},{24,8},{32,16},{40,24},{48,32},{56,40},{64,... | collective-permute-start | bytes 393224 | tf_op jit(solution)/shard_map/ppermute | solution.py:14
  13.1 54.8 %collective-permute-start.3 = (bf16[8,8192]{1,0:T(8,128)(2,1)}, bf16[8,8192]{1,0:T(8,128)(2,1)S(1)}, u32[]{:S(2)}, u32[]{:S(2)}) collective-permute-start(bf16[8,8192]{1,0:T(8,128)(2,1)} %param.32), channel_id=1, source_target_pairs={{0,504},{8,0},{16,8},{24,16},{32,24},{40,32},{48,40},{56,48},{64,5... | collective-permute-start | bytes 393224 | tf_op jit(solution)/shard_map/ppermute | solution.py:14
  15.6 54.0 %collective-permute-start.5 = (bf16[8,8192]{1,0:T(8,128)(2,1)}, bf16[8,8192]{1,0:T(8,128)(2,1)S(1)}, u32[]{:S(2)}, u32[]{:S(2)}) collective-permute-start(bf16[8,8192]{1,0:T(8,128)(2,1)} %param.32), channel_id=1, source_target_pairs={{0,8},{8,16},{16,24},{24,32},{32,40},{40,48},{48,56},{56,64},{64,7... | collective-permute-start | bytes 393224 | tf_op jit(solution)/shard_map/ppermute | solution.py:14
  17.5 53.8 %collective-permute-start.7 = (bf16[8,8192]{1,0:T(8,128)(2,1)}, bf16[8,8192]{1,0:T(8,128)(2,1)S(1)}, u32[]{:S(2)}, u32[]{:S(2)}) collective-permute-start(bf16[8,8192]{1,0:T(8,128)(2,1)} %param.32), channel_id=1, source_target_pairs={{0,16},{8,24},{16,32},{24,40},{32,48},{40,56},{48,64},{56,72},{64,... | collective-permute-start | bytes 393224 | tf_op jit(solution)/shard_map/ppermute | solution.py:14
  24.3 17.2 %collective-permute-start = (s32[129]{0:T(256)S(1)}, s32[129]{0:T(256)S(1)}, u32[]{:S(2)}, u32[]{:S(2)}) collective-permute-start(s32[129]{0:T(256)S(1)} %pad_add_fusion), channel_id=1, source_target_pairs={{0,496},{8,504},{16,0},{24,8},{32,16},{40,24},{48,32},{56,40},{64,... | collective-permute-start | bytes 1556 | tf_op jit(solution)/shard_map/ppermute | solution.py:14
  41.5 5.9 %collective-permute-start.2 = (s32[129]{0:T(256)S(1)}, s32[129]{0:T(256)S(1)}, u32[]{:S(2)}, u32[]{:S(2)}) collective-permute-start(s32[129]{0:T(256)S(1)} %pad_add_fusion.1), channel_id=1, source_target_pairs={{0,504},{8,0},{16,8},{24,16},{32,24},{40,32},{48,40},{56,48},{64,5... | collective-permute-start | bytes 1556 | tf_op jit(solution)/shard_map/ppermute | solution.py:14
  47.4 8.5 %collective-permute-start.4 = (s32[129]{0:T(256)S(1)}, s32[129]{0:T(256)S(1)}, u32[]{:S(2)}, u32[]{:S(2)}) collective-permute-start(s32[129]{0:T(256)S(1)} %pad_add_fusion.2), channel_id=1, source_target_pairs={{0,8},{8,16},{16,24},{24,32},{32,40},{40,48},{48,56},{56,64},{64,7... | collective-permute-start | bytes 1556 | tf_op jit(solution)/shard_map/ppermute | solution.py:14
  55.9 9.1 %collective-permute-start.6 = (s32[129]{0:T(256)S(1)}, s32[129]{0:T(256)S(1)}, u32[]{:S(2)}, u32[]{:S(2)}) collective-permute-start(s32[129]{0:T(256)S(1)} %pad_add_fusion.3), channel_id=1, source_target_pairs={{0,16},{8,24},{16,32},{24,40},{32,48},{40,56},{48,64},{56,72},{64,... | collective-permute-start | bytes 1556 | tf_op jit(solution)/shard_map/ppermute | solution.py:14
  73.7 114.3 %copy-start.1 = (f32[4,32,256]{2,1,0:T(8,128)S(1)}, f32[4,32,256]{2,1,0:T(8,128)}, u32[]{:S(2)}) copy-start(f32[4,32,256]{2,1,0:T(8,128)} %param.36) | copy-start | bytes 393220
  200.9 7.6 %copy-start.6 = (s32[60]{0:T(128)S(1)}, s32[60]{0:T(128)}, u32[]{:S(2)}) copy-start(s32[60]{0:T(128)} %constant.232.clone) | copy-start | bytes 724
  200.9 7.6 %copy-start.5 = (s32[324]{0:T(512)S(1)}, s32[324]{0:T(512)}, u32[]{:S(2)}) copy-start(s32[324]{0:T(512)} %constant.235.clone) | copy-start | bytes 3892
  200.9 21.6 %copy-start.2 = (bf16[9,16,64]{2,1,0:T(8,128)(2,1)S(1)}, bf16[9,16,64]{2,1,0:T(8,128)(2,1)}, u32[]{:S(2)}) copy-start(bf16[9,16,64]{2,1,0:T(8,128)(2,1)} %param.39) | copy-start | bytes 55300
  202.5 11.2 %all-to-all-start = ((bf16[8,32,256]{2,0,1:T(8,128)(2,1)}), bf16[8,32,256]{2,0,1:T(8,128)(2,1)S(1)}, u32[]{:S(2)}, u32[]{:S(2)}) async-start(bf16[8,32,256]{2,0,1:T(8,128)(2,1)} %copy.266), calls=%async_computation | async-start | bytes 262144 | tf_op jit(solution)/shard_map/all_to_all | solution.py:157
  214.6 37.1 %collective-permute-start.8 = (bf16[64,2,60]{0,1,2:T(2,128)(2,1)S(1)}, bf16[64,2,60]{0,1,2:T(2,128)(2,1)S(1)}, u32[]{:S(2)}, u32[]{:S(2)}) collective-permute-start(bf16[64,2,60]{0,1,2:T(2,128)(2,1)S(1)} %get-tuple-element.32), channel_id=1, source_target_pairs={{0,1},{1,2},{2,3},{3,4},{4,5},{5,6},{6,7},{7,8},{8,9},{9,10},{10,1... | collective-permute-start | bytes 46088 | tf_op jit(solution)/shard_map/ppermute | solution.py:24
  217.3 34.5 %collective-permute-start.9 = (bf16[64,2,60]{0,1,2:T(2,128)(2,1)S(1)}, bf16[64,2,60]{0,1,2:T(2,128)(2,1)S(1)}, u32[]{:S(2)}, u32[]{:S(2)}) collective-permute-start(bf16[64,2,60]{0,1,2:T(2,128)(2,1)S(1)} %get-tuple-element.33), channel_id=1, source_target_pairs={{1,0},{2,1},{3,2},{4,3},{5,4},{6,5},{7,6},{8,7},{9,8},{10,9},{11,1... | collective-permute-start | bytes 46088 | tf_op jit(solution)/shard_map/ppermute | solution.py:25
  260.5 10.4 %copy-start.3 = (bf16[9,16,128]{2,1,0:T(8,128)(2,1)S(1)}, bf16[9,16,128]{2,1,0:T(8,128)(2,1)}, u32[]{:S(2)}) copy-start(bf16[9,16,128]{2,1,0:T(8,128)(2,1)} %param.40) | copy-start | bytes 110596
  263.0 39.7 %collective-permute-start.10 = (bf16[128,2,60]{0,1,2:T(2,128)(2,1)S(1)}, bf16[128,2,60]{0,1,2:T(2,128)(2,1)S(1)}, u32[]{:S(2)}, u32[]{:S(2)}) collective-permute-start(bf16[128,2,60]{0,1,2:T(2,128)(2,1)S(1)} %get-tuple-element.30), channel_id=1, source_target_pairs={{0,1},{1,2},{2,3},{3,4},{4,5},{5,6},{6,7},{7,8},{8,9},{9,10},{10,1... | collective-permute-start | bytes 92168 | tf_op jit(solution)/shard_map/ppermute | solution.py:24
  264.9 37.8 %collective-permute-start.11 = (bf16[128,2,60]{0,1,2:T(2,128)(2,1)S(1)}, bf16[128,2,60]{0,1,2:T(2,128)(2,1)S(1)}, u32[]{:S(2)}, u32[]{:S(2)}) collective-permute-start(bf16[128,2,60]{0,1,2:T(2,128)(2,1)S(1)} %get-tuple-element.31), channel_id=1, source_target_pairs={{1,0},{2,1},{3,2},{4,3},{5,4},{6,5},{7,6},{8,7},{9,8},{10,9},{11,1... | collective-permute-start | bytes 92168 | tf_op jit(solution)/shard_map/ppermute | solution.py:25
  309.9 10.4 %copy-start.4 = (bf16[9,16,128]{2,1,0:T(8,128)(2,1)S(1)}, bf16[9,16,128]{2,1,0:T(8,128)(2,1)}, u32[]{:S(2)}) copy-start(bf16[9,16,128]{2,1,0:T(8,128)(2,1)} %param.41) | copy-start | bytes 110596
  312.4 39.7 %collective-permute-start.12 = (bf16[128,2,60]{0,1,2:T(2,128)(2,1)S(1)}, bf16[128,2,60]{0,1,2:T(2,128)(2,1)S(1)}, u32[]{:S(2)}, u32[]{:S(2)}) collective-permute-start(bf16[128,2,60]{0,1,2:T(2,128)(2,1)S(1)} %get-tuple-element.28), channel_id=1, source_target_pairs={{0,1},{1,2},{2,3},{3,4},{4,5},{5,6},{6,7},{7,8},{8,9},{9,10},{10,1... | collective-permute-start | bytes 92168 | tf_op jit(solution)/shard_map/ppermute | solution.py:24
  314.4 37.7 %collective-permute-start.13 = (bf16[128,2,60]{0,1,2:T(2,128)(2,1)S(1)}, bf16[128,2,60]{0,1,2:T(2,128)(2,1)S(1)}, u32[]{:S(2)}, u32[]{:S(2)}) collective-permute-start(bf16[128,2,60]{0,1,2:T(2,128)(2,1)S(1)} %get-tuple-element.29), channel_id=1, source_target_pairs={{1,0},{2,1},{3,2},{4,3},{5,4},{6,5},{7,6},{8,7},{9,8},{10,9},{11,1... | collective-permute-start | bytes 92168 | tf_op jit(solution)/shard_map/ppermute | solution.py:25
where the time goes:
time: 375 us
  local copies, waits for them, and re-layouts  150 us (40%)
  blocking collectives  105 us (28%)
  starting transfers between devices  67.3 us (18%)
  other arithmetic  28.4 us (8%)
  waiting for transfers between devices  14.5 us (4%)
  matrix products  7.92 us (2%)
    gather x1, local copies, waits for them, and re-layouts, on_device(): values = jnp.take(arrived, corner_slot.reshape(-1), axis=1)  114 us
    ppermute x8, starting transfers between devices, from_behind(): return lax.ppermute(value, axis, pairs)  37.5 us
    all_gather x1, blocking collectives, on_device(): lax.all_gather(kernel_three, 'chan', axis=1, tiled=True)  31.7 us
    all_gather x1, blocking collectives, on_device(): lax.all_gather(kernel_two, 'chan', axis=1, tiled=True)  31.7 us
    all_gather x1, blocking collectives, on_device(): lax.all_gather(kernel_one, 'chan', axis=1, tiled=True)  29 us
    ppermute x3, starting transfers between devices, extended_2(): after = lax.ppermute(initial, axis, down)  17.2 us
    reduce_sum x1, other arithmetic, on_device(): jnp.sum(values * corner_weight[None], axis=1).astype(jnp.bfloat16)  13 us
    all_to_all x1, blocking collectives, on_device(): lax.all_to_all(activity, 'chan', split_axis=0, concat_axis=1, tiled=True)  12.5 us
  transfers between devices with their start and end apart: 15, of which 4 were waited for; matrix products, arithmetic and copies ran while one was open for 7% of the time, Pallas kernels for 0%

commit v1 on v0

--- a/solution.py
+++ b/solution.py
@@ -157,7 +157,9 @@
     activity = lax.all_to_all(regridded, "chan", split_axis=1, concat_axis=0, tiled=True)
     kernels = (
         lax.all_gather(kernel_one, "chan", axis=1, tiled=True),
-        lax.all_gather(kernel_two, "chan", axis=1, tiled=True),
+        jnp.concatenate(
+            lax.all_to_all(jnp.stack([kernel_two] * lax.axis_size("chan")), "chan", 0, 0), axis=1
+        ),
         lax.all_gather(kernel_three, "chan", axis=1, tiled=True),
     )
     first_tile = lax.axis_index(("tile", "chan")) * per_group

time: 375 us -> 353 us (0.941)
  blocking collectives: 105 us -> 74.5 us
  starting transfers between devices: 67.3 us -> 72.5 us
    all_gather x1 -> x0, blocking collectives: 31.7 us -> none  [on_device(): lax.all_gather(kernel_two, 'chan', axis=1, tiled=True)]
    all_to_all x0 -> x1, starting transfers between devices: none -> 4.69 us  [on_device(): lax.all_to_all(jnp.stack([kernel_two] * lax.axis_size('chan')), 'chan', 0...]
  transfers between devices with their start and end apart: 15 -> 16, of which waited for: 4 -> 5; matrix products, arithmetic and copies ran while one was open for 7% -> 10% of each run, Pallas kernels for 0% -> 0%
where the time goes in v1:
time: 353 us; the launch traced here: 352 us
  local copies, waits for them, and re-layouts  152 us (43%)
  blocking collectives  74.5 us (21%)
  starting transfers between devices  72.5 us (21%)
  other arithmetic  28.5 us (8%)
  waiting for transfers between devices  15.7 us (4%)
  matrix products  7.92 us (2%)
    gather x1, local copies, waits for them, and re-layouts, on_device(): values = jnp.take(arrived, corner_slot.reshape(-1), axis=1)  115 us
    ppermute x8, starting transfers between devices, from_behind(): return lax.ppermute(value, axis, pairs)  37.5 us
    all_gather x1, blocking collectives, on_device(): lax.all_gather(kernel_three, 'chan', axis=1, tiled=True)  33.1 us
    all_gather x1, blocking collectives, on_device(): lax.all_gather(kernel_one, 'chan', axis=1, tiled=True)  28.9 us
    ppermute x3, starting transfers between devices, extended_2(): after = lax.ppermute(initial, axis, down)  16.1 us
    reduce_sum x1, other arithmetic, on_device(): jnp.sum(values * corner_weight[None], axis=1).astype(jnp.bfloat16)  13 us
    all_to_all x1, blocking collectives, on_device(): lax.all_to_all(activity, 'chan', split_axis=0, concat_axis=1, tiled=True)  12.5 us
    ppermute x8, waiting for transfers between devices, from_behind(): return lax.ppermute(value, axis, pairs)  9.24 us
  transfers between devices with their start and end apart: 16, of which 5 were waited for; matrix products, arithmetic and copies ran while one was open for 10% of the time, Pallas kernels for 0%

profile of v1, /device:TPU:2, one launch (start us, length us, event | category | flops | bytes accessed | tf_op | source)
XLA Modules:
  0.0 352.3 jit_solution(8703543274926659855)
XLA Ops:
  0.0 13.1 %collective-permute-start.1 = (bf16[8,8192]{1,0:T(8,128)(2,1)}, bf16[8,8192]{1,0:T(8,128)(2,1)S(1)}, u32[]{:S(2)}, u32[]{:S(2)}) collective-permute-start(bf16[8,8192]{1,0:T(8,128)(2,1)} %param.32), channel_id=1, source_target_pairs={{0,496},{8,504},{16,0},{24,8},{32,16},{40,24},{48,32},{56,40},{64,... | collective-permute-start | bytes 393224 | tf_op jit(solution)/shard_map/ppermute | solution.py:14
  13.1 2.5 collective-permute-start.3
  15.6 1.9 collective-permute-start.5
  17.5 4.0 %collective-permute-start.7 = (bf16[8,8192]{1,0:T(8,128)(2,1)}, bf16[8,8192]{1,0:T(8,128)(2,1)S(1)}, u32[]{:S(2)}, u32[]{:S(2)}) collective-permute-start(bf16[8,8192]{1,0:T(8,128)(2,1)} %param.32), channel_id=1, source_target_pairs={{0,16},{8,24},{16,32},{24,40},{32,48},{40,56},{48,64},{56,72},{64,... | collective-permute-start | bytes 393224 | tf_op jit(solution)/shard_map/ppermute | solution.py:14
  21.6 1.5 fusion.75
  24.3 5.4 %collective-permute-start = (s32[129]{0:T(256)S(1)}, s32[129]{0:T(256)S(1)}, u32[]{:S(2)}, u32[]{:S(2)}) collective-permute-start(s32[129]{0:T(256)S(1)} %pad_add_fusion), channel_id=1, source_target_pairs={{0,496},{8,504},{16,0},{24,8},{32,16},{40,24},{48,32},{56,40},{64,... | collective-permute-start | bytes 1556 | tf_op jit(solution)/shard_map/ppermute | solution.py:14
  39.0 1.8 copy.262
  41.6 4.6 %collective-permute-start.2 = (s32[129]{0:T(256)S(1)}, s32[129]{0:T(256)S(1)}, u32[]{:S(2)}, u32[]{:S(2)}) collective-permute-start(s32[129]{0:T(256)S(1)} %pad_add_fusion.1), channel_id=1, source_target_pairs={{0,504},{8,0},{16,8},{24,16},{32,24},{40,32},{48,40},{56,48},{64,5... | collective-permute-start | bytes 1556 | tf_op jit(solution)/shard_map/ppermute | solution.py:14
  47.5 4.1 %collective-permute-start.4 = (s32[129]{0:T(256)S(1)}, s32[129]{0:T(256)S(1)}, u32[]{:S(2)}, u32[]{:S(2)}) collective-permute-start(s32[129]{0:T(256)S(1)} %pad_add_fusion.2), channel_id=1, source_target_pairs={{0,8},{8,16},{16,24},{24,32},{32,40},{40,48},{48,56},{56,64},{64,7... | collective-permute-start | bytes 1556 | tf_op jit(solution)/shard_map/ppermute | solution.py:14
  52.8 3.2 collective-permute-done.4
  55.9 1.9 collective-permute-start.6
  59.1 6.0 %collective-permute-done.6 = s32[129]{0:T(256)S(1)} collective-permute-done((s32[129]{0:T(256)S(1)}, s32[129]{0:T(256)S(1)}, u32[]{:S(2)}, u32[]{:S(2)}) %collective-permute-start.6) | collective-permute-done | bytes 548 | tf_op jit(solution)/shard_map/ppermute | solution.py:14
  73.7 115.1 %gather_fusion = bf16[32768,8]{1,0:T(8,128)(2,1)} fusion(bf16[8,640]{0,1:T(8,128)(2,1)S(1)} %fusion.60, s32[32768]{0:T(1024)S(1)} %broadcast_clamp_fusion), kind=kCustom, calls=%fused_computation.13 | custom fusion | bytes 1179648 | tf_op jit(solution)/shard_map/jit(_take)/gather | solution.py:153
  188.8 13.0 %multiply_reduce_fusion = bf16[8,32,256]{0,2,1:T(8,128)(2,1)S(1)} fusion(f32[4,32,256]{2,1,0:T(8,128)S(1)} %copy-done.1, bf16[8,4,32,256]{0,3,2,1:T(8,128)(2,1)} %bitcast.255, pred[4,32,256]{2,1,0:T(8,128)(4,1)S(1)} %compare_and_fusion), kind=kLoop, calls=%fused_computation.17 | loop fusion | flops 983040 | bytes 819200 | tf_op jit(solution)/shard_map/reduce_sum | solution.py:155
  203.5 5.9 %all-to-all-start = ((bf16[8,32,256]{2,0,1:T(8,128)(2,1)}), bf16[8,32,256]{2,0,1:T(8,128)(2,1)S(1)}, u32[]{:S(2)}, u32[]{:S(2)}) async-start(bf16[8,32,256]{2,0,1:T(8,128)(2,1)} %copy.266), calls=%async_computation | async-start | bytes 262144 | tf_op jit(solution)/shard_map/all_to_all | solution.py:157
  209.4 5.2 %all-to-all-done = bf16[8,32,256]{2,0,1:T(8,128)(2,1)S(1)} async-done(((bf16[8,32,256]{2,0,1:T(8,128)(2,1)}), bf16[8,32,256]{2,0,1:T(8,128)(2,1)S(1)}, u32[]{:S(2)}, u32[]{:S(2)}) %all-to-all-start) | async-done | bytes 131104 | tf_op jit(solution)/shard_map/all_to_all | solution.py:157
  215.4 4.7 %all-to-all-start.1 = ((bf16[8,9,16,128]{3,2,1,0:T(8,128)(2,1)}), bf16[8,9,16,128]{3,2,1,0:T(8,128)(2,1)S(1)}, u32[]{:S(2)}, u32[]{:S(2)}) async-start(bf16[8,9,16,128]{3,2,1,0:T(8,128)(2,1)} %stack.2), calls=%async_computation.1 | async-start | bytes 589824 | tf_op jit(solution)/shard_map/all_to_all | solution.py:161
  221.0 3.4 collective-permute-start.8
  224.4 4.6 %collective-permute-start.9 = (bf16[64,2,60]{0,1,2:T(2,128)(2,1)S(1)}, bf16[64,2,60]{0,1,2:T(2,128)(2,1)S(1)}, u32[]{:S(2)}, u32[]{:S(2)}) collective-permute-start(bf16[64,2,60]{0,1,2:T(2,128)(2,1)S(1)} %get-tuple-element.42), channel_id=1, source_target_pairs={{1,0},{2,1},{3,2},{4,3},{5,4},{6,5},{7,6},{8,7},{9,8},{10,9},{11,1... | collective-permute-start | bytes 46088 | tf_op jit(solution)/shard_map/ppermute | solution.py:25
  229.0 28.9 %all_gather.6 = bf16[9,128,64]{2,1,0:T(8,128)(2,1)S(1)} all-gather(bf16[9,16,64]{2,1,0:T(8,128)(2,1)S(1)} %copy-done.3), channel_id=1, replica_groups=mesh['tile'=64,'chan'=8] {'chan'}, dimensions={1}, use_global_device_ids=true | all-gather | bytes 165888 | tf_op jit(solution)/shard_map/all_gather | solution.py:159
  258.2 1.4 gather_fusion.2
  260.0 2.0 gather_fusion.3
  269.2 1.9 collective-permute-start.10
  271.1 6.3 %collective-permute-start.11 = (bf16[128,2,60]{0,1,2:T(2,128)(2,1)S(1)}, bf16[128,2,60]{0,1,2:T(2,128)(2,1)S(1)}, u32[]{:S(2)}, u32[]{:S(2)}) collective-permute-start(bf16[128,2,60]{0,1,2:T(2,128)(2,1)S(1)} %get-tuple-element.40), channel_id=1, source_target_pairs={{1,0},{2,1},{3,2},{4,3},{5,4},{6,5},{7,6},{8,7},{9,8},{10,9},{11,1... | collective-permute-start | bytes 92168 | tf_op jit(solution)/shard_map/ppermute | solution.py:25
  278.9 1.4 gather_fusion.12
  280.8 2.0 gather_fusion.13
  288.4 2.9 collective-permute-start.12
  291.4 5.3 %collective-permute-start.13 = (bf16[128,2,60]{0,1,2:T(2,128)(2,1)S(1)}, bf16[128,2,60]{0,1,2:T(2,128)(2,1)S(1)}, u32[]{:S(2)}, u32[]{:S(2)}) collective-permute-start(bf16[128,2,60]{0,1,2:T(2,128)(2,1)S(1)} %get-tuple-element.38), channel_id=1, source_target_pairs={{1,0},{2,1},{3,2},{4,3},{5,4},{6,5},{7,6},{8,7},{9,8},{10,9},{11,1... | collective-permute-start | bytes 92168 | tf_op jit(solution)/shard_map/ppermute | solution.py:25
  296.7 33.1 %all_gather.7 = bf16[9,128,128]{2,1,0:T(8,128)(2,1)S(1)} all-gather(bf16[9,16,128]{2,1,0:T(8,128)(2,1)S(1)} %copy-done.4), channel_id=1, replica_groups=mesh['tile'=64,'chan'=8] {'chan'}, dimensions={1}, use_global_device_ids=true | all-gather | bytes 331776 | tf_op jit(solution)/shard_map/all_gather | solution.py:163
  330.0 1.4 gather_fusion.15
  332.0 2.0 gather_fusion.16
  338.9 12.5 %all_to_all.41 = bf16[128,4,256]{2,1,0:T(4,128)(2,1)S(1)} all-to-all(bf16[128,4,256]{2,1,0:T(4,128)(2,1)S(1)} %copy.324), channel_id=1, replica_groups=mesh['tile'=64,'chan'=8] {'chan'}, dimensions={0} | all-to-all | bytes 524288 | tf_op jit(solution)/shard_map/all_to_all | solution.py:177
  (176 shorter events, 48.2 us)
Async XLA Ops:
  0.0 34.5 %copy-start = (s32[32,8]{0,1:T(8,128)S(1)}, s32[32,8]{0,1:T(8,128)}, u32[]{:S(2)}) copy-start(s32[32,8]{0,1:T(8,128)} %param.38) | copy-start | bytes 3076
  0.0 66.2 %collective-permute-start.1 = (bf16[8,8192]{1,0:T(8,128)(2,1)}, bf16[8,8192]{1,0:T(8,128)(2,1)S(1)}, u32[]{:S(2)}, u32[]{:S(2)}) collective-permute-start(bf16[8,8192]{1,0:T(8,128)(2,1)} %param.32), channel_id=1, source_target_pairs={{0,496},{8,504},{16,0},{24,8},{32,16},{40,24},{48,32},{56,40},{64,... | collective-permute-start | bytes 393224 | tf_op jit(solution)/shard_map/ppermute | solution.py:14
  13.1 54.9 %collective-permute-start.3 = (bf16[8,8192]{1,0:T(8,128)(2,1)}, bf16[8,8192]{1,0:T(8,128)(2,1)S(1)}, u32[]{:S(2)}, u32[]{:S(2)}) collective-permute-start(bf16[8,8192]{1,0:T(8,128)(2,1)} %param.32), channel_id=1, source_target_pairs={{0,504},{8,0},{16,8},{24,16},{32,24},{40,32},{48,40},{56,48},{64,5... | collective-permute-start | bytes 393224 | tf_op jit(solution)/shard_map/ppermute | solution.py:14
  15.6 54.1 %collective-permute-start.5 = (bf16[8,8192]{1,0:T(8,128)(2,1)}, bf16[8,8192]{1,0:T(8,128)(2,1)S(1)}, u32[]{:S(2)}, u32[]{:S(2)}) collective-permute-start(bf16[8,8192]{1,0:T(8,128)(2,1)} %param.32), channel_id=1, source_target_pairs={{0,8},{8,16},{16,24},{24,32},{32,40},{40,48},{48,56},{56,64},{64,7... | collective-permute-start | bytes 393224 | tf_op jit(solution)/shard_map/ppermute | solution.py:14
  17.5 53.9 %collective-permute-start.7 = (bf16[8,8192]{1,0:T(8,128)(2,1)}, bf16[8,8192]{1,0:T(8,128)(2,1)S(1)}, u32[]{:S(2)}, u32[]{:S(2)}) collective-permute-start(bf16[8,8192]{1,0:T(8,128)(2,1)} %param.32), channel_id=1, source_target_pairs={{0,16},{8,24},{16,32},{24,40},{32,48},{40,56},{48,64},{56,72},{64,... | collective-permute-start | bytes 393224 | tf_op jit(solution)/shard_map/ppermute | solution.py:14
  24.3 17.2 %collective-permute-start = (s32[129]{0:T(256)S(1)}, s32[129]{0:T(256)S(1)}, u32[]{:S(2)}, u32[]{:S(2)}) collective-permute-start(s32[129]{0:T(256)S(1)} %pad_add_fusion), channel_id=1, source_target_pairs={{0,496},{8,504},{16,0},{24,8},{32,16},{40,24},{48,32},{56,40},{64,... | collective-permute-start | bytes 1556 | tf_op jit(solution)/shard_map/ppermute | solution.py:14
  41.6 5.9 %collective-permute-start.2 = (s32[129]{0:T(256)S(1)}, s32[129]{0:T(256)S(1)}, u32[]{:S(2)}, u32[]{:S(2)}) collective-permute-start(s32[129]{0:T(256)S(1)} %pad_add_fusion.1), channel_id=1, source_target_pairs={{0,504},{8,0},{16,8},{24,16},{32,24},{40,32},{48,40},{56,48},{64,5... | collective-permute-start | bytes 1556 | tf_op jit(solution)/shard_map/ppermute | solution.py:14
  47.5 8.5 %collective-permute-start.4 = (s32[129]{0:T(256)S(1)}, s32[129]{0:T(256)S(1)}, u32[]{:S(2)}, u32[]{:S(2)}) collective-permute-start(s32[129]{0:T(256)S(1)} %pad_add_fusion.2), channel_id=1, source_target_pairs={{0,8},{8,16},{16,24},{24,32},{32,40},{40,48},{48,56},{56,64},{64,7... | collective-permute-start | bytes 1556 | tf_op jit(solution)/shard_map/ppermute | solution.py:14
  55.9 9.1 %collective-permute-start.6 = (s32[129]{0:T(256)S(1)}, s32[129]{0:T(256)S(1)}, u32[]{:S(2)}, u32[]{:S(2)}) collective-permute-start(s32[129]{0:T(256)S(1)} %pad_add_fusion.3), channel_id=1, source_target_pairs={{0,16},{8,24},{16,32},{24,40},{32,48},{40,56},{48,64},{56,72},{64,... | collective-permute-start | bytes 1556 | tf_op jit(solution)/shard_map/ppermute | solution.py:14
  73.7 115.1 %copy-start.1 = (f32[4,32,256]{2,1,0:T(8,128)S(1)}, f32[4,32,256]{2,1,0:T(8,128)}, u32[]{:S(2)}) copy-start(f32[4,32,256]{2,1,0:T(8,128)} %param.36) | copy-start | bytes 393220
  201.8 7.6 %copy-start.6 = (s32[60]{0:T(128)S(1)}, s32[60]{0:T(128)}, u32[]{:S(2)}) copy-start(s32[60]{0:T(128)} %constant.232.clone) | copy-start | bytes 724
  201.8 7.6 %copy-start.5 = (s32[324]{0:T(512)S(1)}, s32[324]{0:T(512)}, u32[]{:S(2)}) copy-start(s32[324]{0:T(512)} %constant.235.clone) | copy-start | bytes 3892
  201.8 12.8 %copy-start.2 = (bf16[9,16,128]{2,1,0:T(8,128)(2,1)S(1)}, bf16[9,16,128]{2,1,0:T(8,128)(2,1)}, u32[]{:S(2)}) copy-start(bf16[9,16,128]{2,1,0:T(8,128)(2,1)} %param.40) | copy-start | bytes 110596
  201.9 27.1 %copy-start.3 = (bf16[9,16,64]{2,1,0:T(8,128)(2,1)S(1)}, bf16[9,16,64]{2,1,0:T(8,128)(2,1)}, u32[]{:S(2)}) copy-start(bf16[9,16,64]{2,1,0:T(8,128)(2,1)} %param.39) | copy-start | bytes 55300
  203.5 11.2 %all-to-all-start = ((bf16[8,32,256]{2,0,1:T(8,128)(2,1)}), bf16[8,32,256]{2,0,1:T(8,128)(2,1)S(1)}, u32[]{:S(2)}, u32[]{:S(2)}) async-start(bf16[8,32,256]{2,0,1:T(8,128)(2,1)} %copy.266), calls=%async_computation | async-start | bytes 262144 | tf_op jit(solution)/shard_map/all_to_all | solution.py:157
  215.4 62.0 %all-to-all-start.1 = ((bf16[8,9,16,128]{3,2,1,0:T(8,128)(2,1)}), bf16[8,9,16,128]{3,2,1,0:T(8,128)(2,1)S(1)}, u32[]{:S(2)}, u32[]{:S(2)}) async-start(bf16[8,9,16,128]{3,2,1,0:T(8,128)(2,1)} %stack.2), calls=%async_computation.1 | async-start | bytes 589824 | tf_op jit(solution)/shard_map/all_to_all | solution.py:161
  221.0 37.0 %collective-permute-start.8 = (bf16[64,2,60]{0,1,2:T(2,128)(2,1)S(1)}, bf16[64,2,60]{0,1,2:T(2,128)(2,1)S(1)}, u32[]{:S(2)}, u32[]{:S(2)}) collective-permute-start(bf16[64,2,60]{0,1,2:T(2,128)(2,1)S(1)} %get-tuple-element.41), channel_id=1, source_target_pairs={{0,1},{1,2},{2,3},{3,4},{4,5},{5,6},{6,7},{7,8},{8,9},{9,10},{10,1... | collective-permute-start | bytes 46088 | tf_op jit(solution)/shard_map/ppermute | solution.py:24
  224.4 33.6 %collective-permute-start.9 = (bf16[64,2,60]{0,1,2:T(2,128)(2,1)S(1)}, bf16[64,2,60]{0,1,2:T(2,128)(2,1)S(1)}, u32[]{:S(2)}, u32[]{:S(2)}) collective-permute-start(bf16[64,2,60]{0,1,2:T(2,128)(2,1)S(1)} %get-tuple-element.42), channel_id=1, source_target_pairs={{1,0},{2,1},{3,2},{4,3},{5,4},{6,5},{7,6},{8,7},{9,8},{10,9},{11,1... | collective-permute-start | bytes 46088 | tf_op jit(solution)/shard_map/ppermute | solution.py:25
  269.2 8.2 %collective-permute-start.10 = (bf16[128,2,60]{0,1,2:T(2,128)(2,1)S(1)}, bf16[128,2,60]{0,1,2:T(2,128)(2,1)S(1)}, u32[]{:S(2)}, u32[]{:S(2)}) collective-permute-start(bf16[128,2,60]{0,1,2:T(2,128)(2,1)S(1)} %get-tuple-element.39), channel_id=1, source_target_pairs={{0,1},{1,2},{2,3},{3,4},{4,5},{5,6},{6,7},{7,8},{8,9},{9,10},{10,1... | collective-permute-start | bytes 92168 | tf_op jit(solution)/shard_map/ppermute | solution.py:24
  271.1 7.6 %collective-permute-start.11 = (bf16[128,2,60]{0,1,2:T(2,128)(2,1)S(1)}, bf16[128,2,60]{0,1,2:T(2,128)(2,1)S(1)}, u32[]{:S(2)}, u32[]{:S(2)}) collective-permute-start(bf16[128,2,60]{0,1,2:T(2,128)(2,1)S(1)} %get-tuple-element.40), channel_id=1, source_target_pairs={{1,0},{2,1},{3,2},{4,3},{5,4},{6,5},{7,6},{8,7},{9,8},{10,9},{11,1... | collective-permute-start | bytes 92168 | tf_op jit(solution)/shard_map/ppermute | solution.py:25
  286.0 10.7 %copy-start.4 = (bf16[9,16,128]{2,1,0:T(8,128)(2,1)S(1)}, bf16[9,16,128]{2,1,0:T(8,128)(2,1)}, u32[]{:S(2)}) copy-start(bf16[9,16,128]{2,1,0:T(8,128)(2,1)} %param.41) | copy-start | bytes 110596
  288.4 41.4 %collective-permute-start.12 = (bf16[128,2,60]{0,1,2:T(2,128)(2,1)S(1)}, bf16[128,2,60]{0,1,2:T(2,128)(2,1)S(1)}, u32[]{:S(2)}, u32[]{:S(2)}) collective-permute-start(bf16[128,2,60]{0,1,2:T(2,128)(2,1)S(1)} %get-tuple-element.37), channel_id=1, source_target_pairs={{0,1},{1,2},{2,3},{3,4},{4,5},{5,6},{6,7},{7,8},{8,9},{9,10},{10,1... | collective-permute-start | bytes 92168 | tf_op jit(solution)/shard_map/ppermute | solution.py:24
  291.4 38.5 %collective-permute-start.13 = (bf16[128,2,60]{0,1,2:T(2,128)(2,1)S(1)}, bf16[128,2,60]{0,1,2:T(2,128)(2,1)S(1)}, u32[]{:S(2)}, u32[]{:S(2)}) collective-permute-start(bf16[128,2,60]{0,1,2:T(2,128)(2,1)S(1)} %get-tuple-element.38), channel_id=1, source_target_pairs={{1,0},{2,1},{3,2},{4,3},{5,4},{6,5},{7,6},{8,7},{9,8},{10,9},{11,1... | collective-permute-start | bytes 92168 | tf_op jit(solution)/shard_map/ppermute | solution.py:25
